TPU v7x, 256 devices: a whole 4x4x8 slice. The times are simulated.
256 devices in a mesh: hid: 32 (over z_hi, x, core), wid: 8 (over z_lo, y).
Axes of the slice: x: 4, y: 4, z: 8 (z_hi: 4, z_lo: 2; z = z_hi * 2 + z_lo), core: 2. Of those that a mesh axis runs over, the one named last changes fastest.
Arguments:
- inputs: bfloat16 [768, 8192], P('hid', 'wid'), may hold values from -6 to 6
- gate_weight: bfloat16 [8192, 28672], P('wid', 'hid'), may hold values from -0.0625 to 0.0625
- up_weight: bfloat16 [8192, 28672], P('wid', 'hid'), may hold values from -0.0625 to 0.0625
- down_weight: bfloat16 [28672, 8192], P('hid', 'wid'), may hold values from -0.03125 to 0.03125
- out_grad: bfloat16 [768, 8192], P('hid', 'wid'), may hold values from -0.43164062 to 0.43164062
Outputs:
- input_grad: bfloat16 [768, 8192], P('hid', 'wid')
- gate_grad: bfloat16 [8192, 28672], P('wid', 'hid')
- up_grad: bfloat16 [8192, 28672], P('wid', 'hid')
- down_grad: bfloat16 [28672, 8192], P('hid', 'wid')
All inputs are finite; a program needn't handle non-finite values.
Results may differ from a plain program's by a relative error of at most 0.02.
Values may be sent and summed in bfloat16 or wider, within the bound.
No kernel may reach another device: no remote copies, remote signals or barrier semaphores. Data moves between devices by JAX's collectives and lax.ppermute only.
A program may use at most 64 MiB of HBM per device.

v0:
```python
import jax
import jax.numpy as jnp
from jax import lax
from jax.sharding import PartitionSpec as P


def swiglu_terms(gate, up, hidden_grad):
    sigma = jax.nn.sigmoid(gate)
    hidden = (gate * sigma * up).astype(jnp.bfloat16)
    up_term = (hidden_grad * gate * sigma).astype(jnp.bfloat16)
    gate_term = (hidden_grad * up * sigma * (1.0 + gate * (1.0 - sigma))).astype(jnp.bfloat16)
    return (hidden, gate_term, up_term)


def per_device(inputs, gate_weight, up_weight, down_weight, out_grad):
    all_inputs, all_grads = (
        lax.all_gather(inputs, "hid", axis=0, tiled=True),
        lax.all_gather(out_grad, "hid", axis=0, tiled=True),
    )
    contract_last = (((1,), (1,)), ((), ()))
    gate_part = jnp.dot(all_inputs, gate_weight, preferred_element_type=jnp.float32)
    up_part = jnp.dot(all_inputs, up_weight, preferred_element_type=jnp.float32)
    grad_part = lax.dot_general(
        all_grads, down_weight, contract_last, preferred_element_type=jnp.float32
    )
    gate, up, hidden_grad = (
        lax.psum(gate_part.astype(jnp.bfloat16), "wid").astype(jnp.float32),
        lax.psum(up_part.astype(jnp.bfloat16), "wid").astype(jnp.float32),
        lax.psum(grad_part.astype(jnp.bfloat16), "wid").astype(jnp.float32),
    )
    hidden, gate_term, up_term = swiglu_terms(gate, up, hidden_grad)
    total = lax.dot_general(
        gate_term, gate_weight, contract_last, preferred_element_type=jnp.float32
    )
    input_grad = lax.psum_scatter(
        total
        + lax.dot_general(up_term, up_weight, contract_last, preferred_element_type=jnp.float32),
        "hid",
        scatter_dimension=0,
        tiled=True,
    ).astype(jnp.bfloat16)
    contract_first = (((0,), (0,)), ((), ()))
    gate_grad = lax.dot_general(
        all_inputs, gate_term, contract_first, preferred_element_type=jnp.float32
    ).astype(jnp.bfloat16)
    up_grad = lax.dot_general(
        all_inputs, up_term, contract_first, preferred_element_type=jnp.float32
    ).astype(jnp.bfloat16)
    down_grad = lax.dot_general(
        hidden, all_grads, contract_first, preferred_element_type=jnp.float32
    ).astype(jnp.bfloat16)
    return (input_grad, gate_grad, up_grad, down_grad)


def solution(mesh):
    placed = (P("hid", "wid"), P("wid", "hid"), P("wid", "hid"), P("hid", "wid"), P("hid", "wid"))
    return jax.shard_map(
        per_device,
        mesh=mesh,
        in_specs=placed,
        out_specs=(P("hid", "wid"), P("wid", "hid"), P("wid", "hid"), P("hid", "wid")),
        check_vma=False,
    )
```

profile of v0, /device:TPU:8, one launch (start us, length us, event | category | flops | bytes accessed | tf_op | source)
XLA Modules:
  0.0 344.4 jit_solution(14188217543889474345)
XLA Ops:
  7.2 0.0 copy-start
  7.2 0.0 all-gather.5.cloned.1.call-start
  7.2 0.7 all-gather.5.cloned.1.call-update
  7.9 0.0 all-gather.3.cloned.1.call-start
  8.0 0.7 all-gather.3.cloned.1.call-update
  8.7 0.0 all-reduce.3.cloned.1.call-start
  8.7 57.7 %all-gather.5.cloned.1.call-done = bf16[768,1024]{1,0:T(8,128)(2,1)} async-done(((bf16[24,1024]{1,0:T(8,128)(2,1)}), bf16[768,1024]{1,0:T(8,128)(2,1)}) %all-gather.5.cloned.1.call-update) | async-done | bytes 1572880 | tf_op jit(solution)/shard_map/all_gather | solution.py:17
  66.4 0.0 copy-done
  66.4 0.0 copy-start.5
  66.4 0.0 copy-start.7
  66.4 4.4 %convolution_convert_fusion.1 = bf16[768,896]{1,0:T(8,128)(2,1)} fusion(bf16[768,1024]{1,0:T(8,128)(2,1)} %all-gather.5.cloned.1.call-done, bf16[1024,896]{1,0:T(8,128)(2,1)S(1)} %copy-done), kind=kOutput, calls=%fused_computation.20 | convolution fusion | flops 1409974272 | bytes 4784128 | tf_op jit(solution)/shard_map/dot_general | solution.py:21
  70.8 0.0 copy-done.5
  70.8 0.0 copy-done.7
  70.9 2.9 convolution_convert_fusion.2
  73.7 45.4 %all-gather.3.cloned.1.call-done = bf16[768,1024]{1,0:T(8,128)(2,1)} async-done(((bf16[24,1024]{1,0:T(8,128)(2,1)}), bf16[768,1024]{1,0:T(8,128)(2,1)}) %all-gather.3.cloned.1.call-update) | async-done | bytes 1572880 | tf_op jit(solution)/shard_map/all_gather | solution.py:18
  119.2 4.9 %convolution_convert_fusion.3 = bf16[768,896]{1,0:T(8,128)(2,1)} fusion(bf16[768,1024]{1,0:T(8,128)(2,1)} %all-gather.3.cloned.1.call-done, bf16[896,1024]{1,0:T(8,128)(2,1)} %param.8), kind=kOutput, calls=%fused_computation.22 | convolution fusion | flops 1409974272 | bytes 4784128 | tf_op jit(solution)/shard_map/dot_general | solution.py:23
  124.0 0.0 all-reduce.3.cloned.1.call-update
  124.1 0.2 reduce-scatter.2.cloned.1.call-start
  124.3 104.4 %all-reduce.3.cloned.1.call-done = (bf16[768,896]{1,0:T(8,128)(2,1)}, bf16[768,896]{1,0:T(8,128)(2,1)}, bf16[768,896]{1,0:T(8,128)(2,1)}) async-done(((bf16[768,896]{1,0:T(8,128)(2,1)}, bf16[768,896]{1,0:T(8,128)(2,1)}, bf16[768,896]{1,0:T(8,128)(2,1)}), (bf16[768,896]{1,0:T(8,128)(2,1)}, bf16[768,896]{1,0:T(8,128)(2,1)}, bf16[768,896]{1,0:T(8,128)(2,1)})) %all-reduce.3.cloned.1.call-update) | async-done | bytes 4128784 | tf_op jit(solution)/shard_map/psum | solution.py:28
  228.7 3.4 fusion.2
  232.1 0.0 copy-start.4
  232.1 1.1 copy-done.4
  233.2 0.0 copy-start.2
  233.2 0.0 copy-start.3
  233.2 0.0 copy-start.6
  233.2 1.8 fusion.15
  235.0 0.0 copy-done.2
  235.0 0.0 copy-done.3
  235.0 0.5 copy-done.6
  235.5 3.6 %convolution_add_fusion = f32[768,1024]{1,0:T(8,128)} fusion(f32[768,1024]{1,0:T(8,128)S(1)} %fusion.15, bf16[1024,896]{1,0:T(8,128)(2,1)S(1)} %copy-done.6, bf16[768,896]{1,0:T(8,128)(2,1)S(1)} %copy-done.2, bf16[768,896]{1,0:T(8,128)(2,1)S(1)} %copy-done.3), kind=kOutput, calls=%fused_computation.19 | convolution fusion | flops 1415577600 | bytes 10878976 | tf_op jit(solution)/shard_map/dot_general | solution.py:37
  239.1 0.0 reduce-scatter.2.cloned.1.call-update
  239.1 4.7 %convert_bitcast_fusion.1 = bf16[1024,896]{0,1:T(8,128)(2,1)} fusion(bf16[768,896]{1,0:T(8,128)(2,1)} %copy-done.4, bf16[768,1024]{1,0:T(8,128)(2,1)} %all-gather.5.cloned.1.call-done), kind=kOutput, calls=%fused_computation.17 | convolution fusion | flops 1410203648 | bytes 4784128 | tf_op jit(solution)/shard_map/dot_general | solution.py:43
  243.8 3.8 %copy.9 = bf16[1024,896]{1,0:T(8,128)(2,1)} copy(bf16[1024,896]{0,1:T(8,128)(2,1)} %convert_bitcast_fusion.1) | data formatting | bytes 3670016
  247.6 4.8 %convert_bitcast_fusion = bf16[1024,896]{0,1:T(8,128)(2,1)} fusion(bf16[768,1024]{1,0:T(8,128)(2,1)} %all-gather.5.cloned.1.call-done, bf16[768,896]{1,0:T(8,128)(2,1)S(1)} %copy-done.2, bf16[768,896]{1,0:T(8,128)(2,1)} %get-tuple-element.9), kind=kOutput, calls=%fused_computation.16 | convolution fusion | flops 1415708672 | bytes 6160384 | tf_op jit(solution)/shard_map/dot_general | solution.py:46
  252.4 0.0 copy-start.1
  252.4 3.9 %copy.10 = bf16[1024,896]{1,0:T(8,128)(2,1)} copy(bf16[1024,896]{0,1:T(8,128)(2,1)} %convert_bitcast_fusion) | data formatting | bytes 3670016
  256.3 0.0 copy-done.1
  256.3 4.9 %convolution_convert_fusion = bf16[896,1024]{1,0:T(8,128)(2,1)} fusion(bf16[768,1024]{1,0:T(8,128)(2,1)} %all-gather.3.cloned.1.call-done, bf16[768,896]{1,0:T(8,128)(2,1)S(1)} %copy-done.1, bf16[768,896]{1,0:T(8,128)(2,1)} %get-tuple-element.10), kind=kOutput, calls=%fused_computation.18 | convolution fusion | flops 1415708672 | bytes 6160384 | tf_op jit(solution)/shard_map/dot_general | solution.py:49
  261.2 75.1 %reduce-scatter.2.cloned.1.call-done = f32[24,1024]{1,0:T(8,128)} async-done(((f32[768,1024]{1,0:T(8,128)}), f32[24,1024]{1,0:T(8,128)}) %reduce-scatter.2.cloned.1.call-update) | async-done | bytes 98320 | tf_op jit(solution)/shard_map/reduce_scatter | solution.py:35
  336.3 1.5 convert_element_type.53
Async XLA Ops:
  7.2 59.3 %copy-start = (bf16[1024,896]{1,0:T(8,128)(2,1)S(1)}, bf16[1024,896]{1,0:T(8,128)(2,1)}, u32[]{:S(2)}) copy-start(bf16[1024,896]{1,0:T(8,128)(2,1)} %param.6) | copy-start | bytes 5505028
  7.2 59.2 %all-gather.5.cloned.1.call-start = ((), (), s32[]{:S(2)}) async-start(), calls=%async_computation.2 | async-start | bytes 1622016 | tf_op jit(solution)/shard_map/all_gather | solution.py:17
  7.9 111.3 %all-gather.3.cloned.1.call-start = ((), (), s32[]{:S(2)}) async-start(), calls=%async_computation.1 | async-start | bytes 1622016 | tf_op jit(solution)/shard_map/all_gather | solution.py:18
  8.7 220.0 %all-reduce.3.cloned.1.call-start = ((), (), s32[]{:S(2)}) async-start(), calls=%async_computation.4 | async-start | bytes 8257536 | tf_op jit(solution)/shard_map/psum | solution.py:28
  66.4 4.4 %copy-start.5 = (bf16[1024,896]{1,0:T(8,128)(2,1)S(1)}, bf16[1024,896]{1,0:T(8,128)(2,1)}, u32[]{:S(2)}) copy-start(bf16[1024,896]{1,0:T(8,128)(2,1)} %param.7) | copy-start | bytes 5505028
  66.4 4.4 %copy-start.7 = (bf16[768,1024]{1,0:T(8,128)(2,1)S(1)}, bf16[768,1024]{1,0:T(8,128)(2,1)}, u32[]{:S(2)}) copy-start(bf16[768,1024]{1,0:T(8,128)(2,1)} %all-gather.5.cloned.1.call-done) | copy-start | bytes 4718596
  124.1 212.3 %reduce-scatter.2.cloned.1.call-start = ((), (), s32[]{:S(2)}) async-start(), calls=%async_computation.3 | async-start | bytes 3244032 | tf_op jit(solution)/shard_map/reduce_scatter | solution.py:35
  232.1 1.1 copy-start.4
  233.2 1.8 copy-start.2
  233.2 1.8 copy-start.3
  233.2 2.3 copy-start.6
  252.4 3.9 %copy-start.1 = (bf16[768,896]{1,0:T(8,128)(2,1)S(1)}, bf16[768,896]{1,0:T(8,128)(2,1)}, u32[]{:S(2)}) copy-start(bf16[768,896]{1,0:T(8,128)(2,1)} %get-tuple-element.8) | copy-start | bytes 4128772
Sparse Core Ops, SparseCore 0:
  10.5 55.8 all-gather.4
  69.0 50.1 all-gather.2
  124.2 104.4 all-reduce.2
  239.2 97.0 reduce-scatter.1
where the time goes:
time: 345 us; the launch traced here: 344 us
  waiting for transfers between devices  284 us (82%)
  matrix products  32 us (9%)
  between operations  13.8 us (4%)
  local copies, waits for them, and re-layouts  9.32 us (3%)
  other arithmetic  4.92 us (1%)
    psum x1, waiting for transfers between devices, per_device(): lax.psum(up_part.astype(jnp.bfloat16), 'wid').astype(jnp.float32)  104 us
    reduce_scatter x1, waiting for transfers between devices, per_device(): lax.psum_scatter(total + lax.dot_general(up_term, up_weight, contract_las...  75.1 us
    all_gather x1, waiting for transfers between devices, per_device(): lax.all_gather(inputs, 'hid', axis=0, tiled=True)  57.7 us
    all_gather x1, waiting for transfers between devices, per_device(): lax.all_gather(out_grad, 'hid', axis=0, tiled=True)  45.4 us
    unnamed x18, local copies, waits for them, and re-layouts  9.32 us
  transfers between devices with their start and end apart: 4, of which 4 were waited for; matrix products, arithmetic and copies ran while one was open for 9% of the time, Pallas kernels for 0%

commit v1 on v0

--- a/solution.py
+++ b/solution.py
@@ -15,7 +15,9 @@
 def per_device(inputs, gate_weight, up_weight, down_weight, out_grad):
     all_inputs, all_grads = (
         lax.all_gather(inputs, "hid", axis=0, tiled=True),
-        lax.all_gather(out_grad, "hid", axis=0, tiled=True),
+        jnp.concatenate(
+            lax.all_to_all(jnp.stack([out_grad] * lax.axis_size("hid")), "hid", 0, 0), axis=0
+        ),
     )
     contract_last = (((1,), (1,)), ((), ()))
     gate_part = jnp.dot(all_inputs, gate_weight, preferred_element_type=jnp.float32)

time: 345 us -> 313 us (0.907)
  waiting for transfers between devices: 284 us -> 239 us
  starting transfers between devices: 0.34 us -> 11.6 us
    all_gather x1 -> x0, waiting for transfers between devices: 45.4 us -> none  [per_device(): lax.all_gather(out_grad, 'hid', axis=0, tiled=True)]
    all_to_all x0 -> x1, waiting for transfers between devices: none -> 40.9 us  [per_device(): lax.all_to_all(jnp.stack([out_grad] * lax.axis_size('hid')), 'hid', 0, 0)]
    all_gather x1, waiting for transfers between devices: 57.7 us -> 17.8 us  [per_device(): lax.all_gather(inputs, 'hid', axis=0, tiled=True)]
    all_to_all x0 -> x1, starting transfers between devices: none -> 11.3 us  [per_device(): lax.all_to_all(jnp.stack([out_grad] * lax.axis_size('hid')), 'hid', 0, 0)]
    unnamed x18 -> x16, local copies, waits for them, and re-layouts: 9.32 us -> 9.19 us
where the time goes in v1:
time: 313 us; the launch traced here: 312 us
  waiting for transfers between devices  239 us (76%)
  matrix products  31.8 us (10%)
  between operations  13.8 us (4%)
  starting transfers between devices  11.6 us (4%)
  local copies, waits for them, and re-layouts  11.5 us (4%)
  other arithmetic  4.92 us (2%)
    psum x1, waiting for transfers between devices, per_device(): lax.psum(up_part.astype(jnp.bfloat16), 'wid').astype(jnp.float32)  104 us
    reduce_scatter x1, waiting for transfers between devices, per_device(): lax.psum_scatter(total + lax.dot_general(up_term, up_weight, contract_las...  74.9 us
    all_to_all x1, waiting for transfers between devices, per_device(): lax.all_to_all(jnp.stack([out_grad] * lax.axis_size('hid')), 'hid', 0, 0)  40.9 us
    all_gather x1, waiting for transfers between devices, per_device(): lax.all_gather(inputs, 'hid', axis=0, tiled=True)  17.8 us
    all_to_all x1, starting transfers between devices, per_device(): lax.all_to_all(jnp.stack([out_grad] * lax.axis_size('hid')), 'hid', 0, 0)  11.3 us
    unnamed x16, local copies, waits for them, and re-layouts  9.19 us
  transfers between devices with their start and end apart: 4, of which 4 were waited for; matrix products, arithmetic and copies ran while one was open for 9% of the time, Pallas kernels for 0%

profile of v1, /device:TPU:8, one launch (start us, length us, event | category | flops | bytes accessed | tf_op | source)
XLA Modules:
  0.0 312.2 jit_solution(18145956979004753303)
XLA Ops:
  7.2 0.0 copy-start
  7.2 2.3 stack.2
  9.4 11.3 %all-to-all-start = ((bf16[32,24,1024]{2,1,0:T(8,128)(2,1)}), bf16[32,24,1024]{2,1,0:T(8,128)(2,1)S(1)}, u32[]{:S(2)}, u32[]{:S(2)}) async-start(bf16[32,24,1024]{2,1,0:T(8,128)(2,1)} %stack.2), calls=%async_computation | async-start | bytes 3145728 | tf_op jit(solution)/shard_map/all_to_all | solution.py:19
  20.8 0.0 all-gather.2.cloned.1.call-start
  20.8 0.7 all-gather.2.cloned.1.call-update
  21.5 0.0 all-reduce.3.cloned.1.call-start
  21.6 40.9 %all-to-all-done = bf16[32,24,1024]{2,1,0:T(8,128)(2,1)S(1)} async-done(((bf16[32,24,1024]{2,1,0:T(8,128)(2,1)}), bf16[32,24,1024]{2,1,0:T(8,128)(2,1)S(1)}, u32[]{:S(2)}, u32[]{:S(2)}) %all-to-all-start) | async-done | bytes 1572896 | tf_op jit(solution)/shard_map/all_to_all | solution.py:19
  62.4 4.4 %convolution_convert_fusion.3 = bf16[768,896]{1,0:T(8,128)(2,1)} fusion(bf16[768,1024]{1,0:T(8,128)(2,1)S(1)} %bitcast.18, bf16[896,1024]{1,0:T(8,128)(2,1)} %param.8), kind=kOutput, calls=%fused_computation.22 | convolution fusion | flops 1409974272 | bytes 4784128 | tf_op jit(solution)/shard_map/dot_general | solution.py:25
  66.8 17.8 %all-gather.2.cloned.1.call-done = bf16[768,1024]{1,0:T(8,128)(2,1)} async-done(((bf16[24,1024]{1,0:T(8,128)(2,1)}), bf16[768,1024]{1,0:T(8,128)(2,1)}) %all-gather.2.cloned.1.call-update) | async-done | bytes 1572880 | tf_op jit(solution)/shard_map/all_gather | solution.py:17
  84.6 0.0 copy-done
  84.6 0.0 copy-start.4
  84.6 0.0 copy-start.6
  84.6 4.4 %convolution_convert_fusion.1 = bf16[768,896]{1,0:T(8,128)(2,1)} fusion(bf16[768,1024]{1,0:T(8,128)(2,1)} %all-gather.2.cloned.1.call-done, bf16[1024,896]{1,0:T(8,128)(2,1)S(1)} %copy-done), kind=kOutput, calls=%fused_computation.20 | convolution fusion | flops 1409974272 | bytes 4784128 | tf_op jit(solution)/shard_map/dot_general | solution.py:23
  89.0 0.0 copy-done.4
  89.0 0.0 copy-done.6
  89.0 2.9 convolution_convert_fusion.2
  91.9 0.0 all-reduce.3.cloned.1.call-update
  91.9 0.2 reduce-scatter.2.cloned.1.call-start
  92.2 104.4 %all-reduce.3.cloned.1.call-done = (bf16[768,896]{1,0:T(8,128)(2,1)}, bf16[768,896]{1,0:T(8,128)(2,1)}, bf16[768,896]{1,0:T(8,128)(2,1)}) async-done(((bf16[768,896]{1,0:T(8,128)(2,1)}, bf16[768,896]{1,0:T(8,128)(2,1)}, bf16[768,896]{1,0:T(8,128)(2,1)}), (bf16[768,896]{1,0:T(8,128)(2,1)}, bf16[768,896]{1,0:T(8,128)(2,1)}, bf16[768,896]{1,0:T(8,128)(2,1)})) %all-reduce.3.cloned.1.call-update) | async-done | bytes 4128784 | tf_op jit(solution)/shard_map/psum | solution.py:30
  196.5 3.4 %fusion.2 = bf16[768,896]{1,0:T(8,128)(2,1)S(1)} fusion(bf16[768,896]{1,0:T(8,128)(2,1)} %get-tuple-element.8, bf16[768,896]{1,0:T(8,128)(2,1)} %get-tuple-element.9, bf16[768,896]{1,0:T(8,128)(2,1)} %get-tuple-element.10), kind=kLoop, calls=%fused_computation.8 | loop fusion | flops 8945664 | bytes 5505024 | tf_op jit(solution)/shard_map/convert_element_type | solution.py:11
  199.9 0.0 copy-start.3
  199.9 1.1 copy-done.3
  201.0 0.0 copy-start.1
  201.0 0.0 copy-start.2
  201.0 0.0 copy-start.5
  201.0 1.8 fusion.15
  202.9 0.0 copy-done.1
  202.9 0.0 copy-done.2
  202.9 0.5 copy-done.5
  203.4 3.5 %convolution_add_fusion = f32[768,1024]{1,0:T(8,128)} fusion(f32[768,1024]{1,0:T(8,128)S(1)} %fusion.15, bf16[1024,896]{1,0:T(8,128)(2,1)S(1)} %copy-done.5, bf16[768,896]{1,0:T(8,128)(2,1)S(1)} %copy-done.1, bf16[768,896]{1,0:T(8,128)(2,1)S(1)} %copy-done.2), kind=kOutput, calls=%fused_computation.19 | convolution fusion | flops 1415577600 | bytes 10878976 | tf_op jit(solution)/shard_map/dot_general | solution.py:39
  206.9 0.0 reduce-scatter.2.cloned.1.call-update
  206.9 4.7 %convert_bitcast_fusion.1 = bf16[1024,896]{0,1:T(8,128)(2,1)} fusion(bf16[768,896]{1,0:T(8,128)(2,1)} %copy-done.3, bf16[768,1024]{1,0:T(8,128)(2,1)} %all-gather.2.cloned.1.call-done), kind=kOutput, calls=%fused_computation.17 | convolution fusion | flops 1410203648 | bytes 4784128 | tf_op jit(solution)/shard_map/dot_general | solution.py:45
  211.6 3.8 %copy.9 = bf16[1024,896]{1,0:T(8,128)(2,1)} copy(bf16[1024,896]{0,1:T(8,128)(2,1)} %convert_bitcast_fusion.1) | data formatting | bytes 3670016
  215.4 5.2 %convert_bitcast_fusion = bf16[1024,896]{0,1:T(8,128)(2,1)} fusion(bf16[768,1024]{1,0:T(8,128)(2,1)} %all-gather.2.cloned.1.call-done, bf16[768,896]{1,0:T(8,128)(2,1)} %get-tuple-element.10, bf16[768,896]{1,0:T(8,128)(2,1)} %get-tuple-element.9), kind=kOutput, calls=%fused_computation.16 | convolution fusion | flops 1415708672 | bytes 6160384 | tf_op jit(solution)/shard_map/dot_general | solution.py:48
  220.6 3.8 %copy.10 = bf16[1024,896]{1,0:T(8,128)(2,1)} copy(bf16[1024,896]{0,1:T(8,128)(2,1)} %convert_bitcast_fusion) | data formatting | bytes 3670016
  224.4 4.8 %convolution_convert_fusion = bf16[896,1024]{1,0:T(8,128)(2,1)} fusion(bf16[768,1024]{1,0:T(8,128)(2,1)S(1)} %bitcast.19, bf16[768,896]{1,0:T(8,128)(2,1)} %get-tuple-element.8, bf16[768,896]{1,0:T(8,128)(2,1)} %get-tuple-element.10), kind=kOutput, calls=%fused_computation.18 | convolution fusion | flops 1415708672 | bytes 6160384 | tf_op jit(solution)/shard_map/dot_general | solution.py:51
  229.3 74.9 %reduce-scatter.2.cloned.1.call-done = f32[24,1024]{1,0:T(8,128)} async-done(((f32[768,1024]{1,0:T(8,128)}), f32[24,1024]{1,0:T(8,128)}) %reduce-scatter.2.cloned.1.call-update) | async-done | bytes 98320 | tf_op jit(solution)/shard_map/reduce_scatter | solution.py:37
  304.2 1.5 convert_element_type.53
Async XLA Ops:
  7.2 77.4 %copy-start = (bf16[1024,896]{1,0:T(8,128)(2,1)S(1)}, bf16[1024,896]{1,0:T(8,128)(2,1)}, u32[]{:S(2)}) copy-start(bf16[1024,896]{1,0:T(8,128)(2,1)} %param.6) | copy-start | bytes 5505028
  9.4 53.0 %all-to-all-start = ((bf16[32,24,1024]{2,1,0:T(8,128)(2,1)}), bf16[32,24,1024]{2,1,0:T(8,128)(2,1)S(1)}, u32[]{:S(2)}, u32[]{:S(2)}) async-start(bf16[32,24,1024]{2,1,0:T(8,128)(2,1)} %stack.2), calls=%async_computation | async-start | bytes 3145728 | tf_op jit(solution)/shard_map/all_to_all | solution.py:19
  20.8 63.8 %all-gather.2.cloned.1.call-start = ((), (), s32[]{:S(2)}) async-start(), calls=%async_computation.2 | async-start | bytes 1622016 | tf_op jit(solution)/shard_map/all_gather | solution.py:17
  21.5 175.0 %all-reduce.3.cloned.1.call-start = ((), (), s32[]{:S(2)}) async-start(), calls=%async_computation.4 | async-start | bytes 8257536 | tf_op jit(solution)/shard_map/psum | solution.py:30
  84.6 4.4 %copy-start.4 = (bf16[1024,896]{1,0:T(8,128)(2,1)S(1)}, bf16[1024,896]{1,0:T(8,128)(2,1)}, u32[]{:S(2)}) copy-start(bf16[1024,896]{1,0:T(8,128)(2,1)} %param.7) | copy-start | bytes 5505028
  84.6 4.4 %copy-start.6 = (bf16[768,1024]{1,0:T(8,128)(2,1)S(1)}, bf16[768,1024]{1,0:T(8,128)(2,1)}, u32[]{:S(2)}) copy-start(bf16[768,1024]{1,0:T(8,128)(2,1)} %all-gather.2.cloned.1.call-done) | copy-start | bytes 4718596
  91.9 212.2 %reduce-scatter.2.cloned.1.call-start = ((), (), s32[]{:S(2)}) async-start(), calls=%async_computation.3 | async-start | bytes 3244032 | tf_op jit(solution)/shard_map/reduce_scatter | solution.py:37
  199.9 1.1 copy-start.3
  201.0 1.8 copy-start.1
  201.0 1.8 copy-start.2
  201.0 2.3 copy-start.5
Sparse Core Ops, SparseCore 0:
  24.1 60.4 all-gather.1
  92.0 104.4 all-reduce.2
  207.0 97.0 reduce-scatter.1
